TPU v7x, 256 devices: a whole 4x4x8 slice. The times are simulated.
256 devices in a mesh: section: 2 (over core), seq: 32 (over z, x), cfg: 4 (over y).
Axes of the slice: x: 4, y: 4, z: 8, core: 2. Of those that a mesh axis runs over, the one named last changes fastest.
Arguments:
- hidden_states: bfloat16 [4, 4, 512, 3072], P('cfg', None, 'seq'), may hold values from -250 to 250
- latent: float32 [2, 4, 512, 64], P('section', None, 'seq'), may hold values from -6 to 6
- stale_cache: bfloat16 [2, 4, 32, 2048, 128], P('section', 'cfg', 'seq'), may hold values from -140 to 140
- qkv_weight: bfloat16 [2, 3072, 3, 2048], P('section', None, None, 'cfg'), may hold values from -0.109375 to 0.109375
- out_weight: bfloat16 [2, 3072, 2048], P('section', 'seq', 'cfg'), may hold values from -0.125 to 0.125
- modulation: float32 [2, 6, 3072], P('section'), may hold values from -2.5 to 2.5
- out_modulation: float32 [2, 3072], replicated, may hold values from -2.5 to 2.5
- proj_weight: bfloat16 [3072, 64], replicated, may hold values from -0.109375 to 0.109375
- solver_coef: float32 [2, 3], P('section'), may hold values from 0.5 to 2
- video_len: int32 [2], replicated, may hold values from 911 to 1822, as said below
- text_len: int32 [4], replicated, may hold values from 1 to 226, as said below
- positions: int32 [3, 2, 4, 512], P(None, None, None, 'seq'), may hold values from 0 to 47
Outputs:
- new_latent: float32 [2, 4, 512, 64], P('section', None, 'seq')
- new_cache: bfloat16 [2, 4, 32, 2048, 128], P('section', 'cfg', 'seq')
Inputs may be any that keep to these rules, and one draw needn't show every extreme that they name: `video_len`: in every draw one request has exactly 1822 video tokens. `text_len`: in every draw some sequence has all 226 text tokens live.
All inputs are finite; a program needn't handle non-finite values.
Results may differ from a plain program's by a relative error of at most 0.02.
Values may be sent and summed in bfloat16 or wider, within the bound.
No kernel may reach another device: no remote copies, remote signals or barrier semaphores. Data moves between devices by JAX's collectives and lax.ppermute only.
A program may use at most 128 MiB of HBM per device.

v0:
```python
import math

import jax
import jax.numpy as jnp
from jax import lax
from jax.sharding import PartitionSpec as P

HD = 64
TEXT = 226


def from_behind(value, axis, steps):
    count = lax.axis_size(axis)
    pairs = [(source, (source + steps) % count) for source in range(count)]
    return lax.ppermute(value, axis, pairs)


def row_norm(values):
    centered = values - jnp.mean(values, axis=-1, keepdims=True)
    return centered * lax.rsqrt(jnp.mean(centered * centered, axis=-1, keepdims=True) + 1e-05)


def head_norm(values):
    centered = values - jnp.mean(values, axis=-1, keepdims=True)
    return centered * lax.rsqrt(jnp.mean(centered * centered, axis=-1, keepdims=True) + 1e-06)


def rope_angles(places, head_size):
    half_size = head_size // 2
    pairs_t = head_size // 8
    pairs_h = (half_size - pairs_t) // 2
    pair_index = jnp.arange(half_size)
    first_part = pair_index < pairs_t
    second_part = jnp.logical_and(pair_index >= pairs_t, pair_index < pairs_t + pairs_h)
    third_part = pair_index >= pairs_t + pairs_h
    local_index = jnp.where(
        first_part,
        pair_index,
        jnp.where(second_part, pair_index - pairs_t, pair_index - pairs_t - pairs_h),
    )
    axis_span = jnp.where(first_part, 2 * pairs_t, 2 * pairs_h)
    frequency = jnp.exp(
        -math.log(10000.0) * 2.0 * local_index.astype(jnp.float32) / axis_span.astype(jnp.float32)
    )
    angles = places[0][..., None] * first_part.astype(jnp.float32)
    angles = angles + places[1][..., None] * second_part.astype(jnp.float32)
    angles = angles + places[2][..., None] * third_part.astype(jnp.float32)
    return angles * frequency


def rotate(values, cos_table, sin_table):
    half_size = values.shape[-1] // 2
    first_half = values[..., :half_size]
    second_half = values[..., half_size:]
    return jnp.concatenate(
        [
            first_half * cos_table - second_half * sin_table,
            second_half * cos_table + first_half * sin_table,
        ],
        axis=-1,
    )


def spread(values):
    return lax.all_gather(values, "cfg", axis=0, tiled=True)


def handoff(values):
    return from_behind(values, "section", 1)


def per_device(
    hidden_states,
    latent,
    stale_cache,
    qkv_weight,
    out_weight,
    modulation,
    out_modulation,
    proj_weight,
    solver_coef,
    video_len,
    text_len,
    positions,
):
    section_id = lax.axis_index("section")
    shard_id = lax.axis_index("seq")
    seq_devices = lax.axis_size("seq")
    patches = hidden_states.shape[1]
    patch_dev = hidden_states.shape[2]
    width = hidden_states.shape[3]
    patch_len = patch_dev * seq_devices
    total_len = patch_len * patches
    group_heads = qkv_weight.shape[3] // HD
    qkv_full = qkv_weight[0].reshape(width, 3, group_heads, HD)
    out_full = lax.all_gather(out_weight[0], "seq", axis=0, tiled=True).reshape(
        width, group_heads, HD
    )
    mod_rows = modulation[0]
    stale_rows = stale_cache[0, 0, 0]
    my_sequence = shard_id // group_heads
    row_ids = jnp.arange(total_len)
    text_limit = lax.dynamic_index_in_dim(text_len, my_sequence, keepdims=False)
    video_limit = lax.dynamic_index_in_dim(video_len, my_sequence // 2, keepdims=False)
    live_keys = jnp.where(row_ids < TEXT, row_ids < text_limit, row_ids - TEXT < video_limit)
    key_patch = row_ids // patch_len
    query_block = patch_len
    while query_block > 1024 and query_block % 2 == 0:
        query_block = query_block // 2
    scale_factor = HD ** (-0.5)
    key_cache = stale_rows
    received = jnp.zeros_like(hidden_states[:, :1])
    pieces = []
    for tick_id in range(patches + 1):
        first_patch = jnp.clip(tick_id - section_id, 0, patches - 1)
        source = hidden_states[:, min(tick_id, patches - 1)][:, None]
        hidden = jnp.where(section_id == 0, source, received)
        run_key_cache = key_cache
        patch_count = hidden.shape[1]
        row_place = (
            (first_patch + jnp.arange(patch_count))[:, None] * patch_len
            + shard_id * patch_dev
            + jnp.arange(patch_dev)[None, :]
        )
        text_rows = (row_place < TEXT)[:, :, None]
        run_normed = row_norm(hidden.astype(jnp.float32))
        shift_rows = jnp.where(text_rows, mod_rows[3], mod_rows[0])
        scale_rows = jnp.where(text_rows, mod_rows[4], mod_rows[1])
        gate_rows = jnp.where(text_rows, mod_rows[5], mod_rows[2])
        mixed_rows = (run_normed * (1.0 + scale_rows) + shift_rows).astype(jnp.bfloat16)
        mixed_rows = spread(mixed_rows)
        seq_count = mixed_rows.shape[0]
        projected = jnp.einsum(
            "spqd,djge->sgjpqe", mixed_rows, qkv_full, preferred_element_type=jnp.float32
        )
        places = lax.dynamic_slice_in_dim(positions, first_patch, patch_count, 2).astype(
            jnp.float32
        )
        angles = rope_angles(places, HD)
        angles = jnp.where(text_rows[None], 0.0, angles)
        angles = jnp.repeat(angles, 2, axis=0)[:, None]
        cos_table = jnp.cos(angles)
        sin_table = jnp.sin(angles)
        queries = rotate(head_norm(projected[:, :, 0]), cos_table, sin_table)
        key_part = rotate(head_norm(projected[:, :, 1]), cos_table, sin_table)
        stacked = jnp.stack([queries, key_part, projected[:, :, 2]], axis=2).astype(jnp.bfloat16)
        outgoing = stacked.reshape(seq_count * group_heads, 3, patch_count, patch_dev * HD)
        incoming = lax.all_to_all(outgoing, "seq", split_axis=0, concat_axis=3, tiled=True)
        incoming = incoming.reshape(3, patch_count * patch_len, HD)
        fresh_rows = jnp.concatenate([incoming[1], incoming[2]], axis=-1)
        run_key_cache = lax.dynamic_update_slice_in_dim(
            run_key_cache, fresh_rows, first_patch * patch_len, 0
        )
        block_count = patch_count * patch_len // query_block

        def attend(work_item):
            query_rows, block_id = work_item
            patch_now = first_patch + block_id * query_block // patch_len
            key_rows = jnp.where((key_patch <= patch_now)[:, None], run_key_cache, stale_rows)
            scores = (
                jnp.dot(query_rows, key_rows[:, :HD].T, preferred_element_type=jnp.float32)
                * scale_factor
            )
            scores = jnp.where(live_keys[None, :], scores, -jnp.inf)
            row_max = jnp.max(scores, axis=1, keepdims=True)
            weights = jnp.exp(scores - row_max)
            row_sum = jnp.sum(weights, axis=1, keepdims=True)
            combined = jnp.dot(
                weights.astype(jnp.bfloat16), key_rows[:, HD:], preferred_element_type=jnp.float32
            )
            return (combined / row_sum).astype(jnp.bfloat16)

        attended = lax.map(
            attend, (incoming[0].reshape(block_count, query_block, HD), jnp.arange(block_count))
        )
        attended = attended.reshape(patch_count, seq_devices, patch_dev * HD)[None]
        returned = lax.all_to_all(attended, "seq", split_axis=2, concat_axis=0, tiled=True)
        returned = returned.reshape(seq_count, group_heads, patch_count, patch_dev, HD)
        update = lax.psum_scatter(
            jnp.einsum("sgpqe,dge->spqd", returned, out_full, preferred_element_type=jnp.float32),
            "cfg",
            scatter_dimension=0,
            tiled=True,
        )
        result = (hidden.astype(jnp.float32) + gate_rows * update).astype(jnp.bfloat16)
        result, key_cache = (result, run_key_cache)
        received = handoff(result)
        if tick_id > 0:
            final_rows = jnp.where(section_id == 1, result, received)
            normed = row_norm(final_rows.astype(jnp.float32))
            normed_out = (normed * (1.0 + out_modulation[1]) + out_modulation[0]).astype(
                jnp.bfloat16
            )
            normed_all = spread(normed_out)
            pair_rows = lax.dynamic_slice_in_dim(normed_all, 2 * section_id, 2, 0)[:, 0]
            predicted = jnp.einsum(
                "sqd,do->sqo", pair_rows, proj_weight, preferred_element_type=jnp.float32
            )
            solver_row = solver_coef[0]
            guided = predicted[0] + solver_row[2] * (predicted[1] - predicted[0])
            pieces.append(solver_row[0] * latent[0, tick_id - 1] + solver_row[1] * guided)
    new_latent = jnp.stack(pieces, axis=0)[None]
    return (new_latent, key_cache[None, None, None])


def solution(mesh):
    return jax.shard_map(
        per_device,
        mesh=mesh,
        in_specs=(
            P("cfg", None, "seq", None),
            P("section", None, "seq", None),
            P("section", "cfg", "seq", None, None),
            P("section", None, None, "cfg"),
            P("section", "seq", "cfg"),
            P("section", None, None),
            P(),
            P(),
            P("section", None),
            P(),
            P(),
            P(None, None, None, "seq"),
        ),
        out_specs=(P("section", None, "seq", None), P("section", "cfg", "seq", None, None)),
        check_vma=False,
    )
```

profile of v0, /device:TPU:2, one launch (start us, length us, event | category | flops | bytes accessed | tf_op | source)
XLA Modules:
  0.0 681.2 jit_solution(16365151907366130737)
XLA Ops:
  12.5 13.0 %all_gather.30 = bf16[4,1,16,3072]{3,2,1,0:T(8,128)(2,1)S(1)} all-gather(bf16[1,1,16,3072]{3,2,1,0:T(8,128)(2,1)S(1)} %fusion.169), channel_id=1, replica_groups=mesh['section'=2,'seq'=32,'cfg'=4] {'cfg'}, dimensions={0}, use_global_device_ids=true | all-gather | bytes 491520 | tf_op jit(solution)/shard_map/all_gather | solution.py:65
  25.6 12.7 %copy.108 = bf16[1,3072,3,512]{1,3,2,0:T(8,128)(2,1)} copy(bf16[1,3072,3,512]{3,1,2,0:T(8,128)(2,1)} %param.15) | data formatting | bytes 18874368 | tf_op args[3]
  38.3 7.1 %convolution_bitcast_fusion.9 = f32[4,8,3,1,16,64]{5,4,1,2,0,3:T(8,128)S(1)} fusion(bf16[3072,3,8,64,1]{0,3,2,1,4:T(8,128)(2,1)} %bitcast.381, bf16[4,1,16,3072]{3,2,1,0:T(8,128)(2,1)S(1)} %all_gather.30), kind=kOutput, calls=%fused_computation.44 | convolution fusion | flops 603979776 | bytes 10223616 | tf_op jit(solution)/shard_map/spqd,djge->sgjpqe/dot_general | solution.py:133
  50.8 11.6 %all-to-all-start = ((bf16[32,3,1,1024]{3,1,2,0:T(4,128)(2,1)}), bf16[32,3,1,1024]{3,1,2,0:T(4,128)(2,1)S(1)}, u32[]{:S(2)}, u32[]{:S(2)}) async-start(bf16[32,3,1,1024]{3,1,2,0:T(4,128)(2,1)} %pad_maximum_fusion), calls=%async_computation | async-start | bytes 524288 | tf_op jit(solution)/shard_map/all_to_all | solution.py:148
  65.1 9.8 %all-to-all-done = bf16[32,3,1,1024]{3,1,2,0:T(4,128)(2,1)S(1)} async-done(((bf16[32,3,1,1024]{3,1,2,0:T(4,128)(2,1)}), bf16[32,3,1,1024]{3,1,2,0:T(4,128)(2,1)S(1)}, u32[]{:S(2)}, u32[]{:S(2)}) %all-to-all-start) | async-done | bytes 196640 | tf_op jit(solution)/shard_map/all_to_all | solution.py:148
  81.3 13.8 %all_to_all.120 = bf16[32,2,512]{2,1,0:T(2,128)(2,1)S(1)} all-to-all(bf16[32,2,512]{2,1,0:T(2,128)(2,1)S(1)} %reshape.2908), channel_id=1, replica_groups=mesh['section'=2,'seq'=32,'cfg'=4] {'seq'}, dimensions={0} | all-to-all | bytes 131072 | tf_op jit(solution)/shard_map/all_to_all | solution.py:177
  104.5 18.6 %reduce-scatter.6.cloned.1.call-done = f32[1,1,16,3072]{3,2,0,1:T(8,128)} async-done(((f32[4,1,16,3072]{3,2,0,1:T(8,128)}), f32[1,1,16,3072]{3,2,0,1:T(8,128)}) %reduce-scatter.6.cloned.1.call-update) | async-done | bytes 196624 | tf_op jit(solution)/shard_map/reduce_scatter | solution.py:179
  128.1 13.0 %all_gather.32 = bf16[4,1,16,3072]{3,2,1,0:T(8,128)(2,1)S(1)} all-gather(bf16[1,1,16,3072]{3,2,1,0:T(8,128)(2,1)S(1)} %fusion.170), channel_id=1, replica_groups=mesh['section'=2,'seq'=32,'cfg'=4] {'cfg'}, dimensions={0}, use_global_device_ids=true | all-gather | bytes 491520 | tf_op jit(solution)/shard_map/all_gather | solution.py:65
  160.6 10.2 %all-to-all-start.2 = ((bf16[32,3,1,1024]{3,1,2,0:T(4,128)(2,1)}), bf16[32,3,1,1024]{3,1,2,0:T(4,128)(2,1)}, u32[]{:S(2)}, u32[]{:S(2)}) async-start(bf16[32,3,1,1024]{3,1,2,0:T(4,128)(2,1)} %pad_maximum_fusion.1), calls=%async_computation.3 | async-start | bytes 524288 | tf_op jit(solution)/shard_map/all_to_all | solution.py:148
  171.4 9.3 %all-to-all-done.2 = bf16[32,3,1,1024]{3,1,2,0:T(4,128)(2,1)} async-done(((bf16[32,3,1,1024]{3,1,2,0:T(4,128)(2,1)}), bf16[32,3,1,1024]{3,1,2,0:T(4,128)(2,1)}, u32[]{:S(2)}, u32[]{:S(2)}) %all-to-all-start.2) | async-done | bytes 196640 | tf_op jit(solution)/shard_map/all_to_all | solution.py:148
  203.3 15.7 %all_to_all.121 = bf16[32,2,512]{2,1,0:T(2,128)(2,1)} all-to-all(bf16[32,2,512]{2,1,0:T(2,128)(2,1)} %reshape.2910), channel_id=1, replica_groups=mesh['section'=2,'seq'=32,'cfg'=4] {'seq'}, dimensions={0} | all-to-all | bytes 131072 | tf_op jit(solution)/shard_map/all_to_all | solution.py:177
  226.6 19.3 %reduce-scatter.8.cloned.1.call-done = f32[1,1,16,3072]{3,2,0,1:T(8,128)} async-done(((f32[4,1,16,3072]{3,2,0,1:T(8,128)}), f32[1,1,16,3072]{3,2,0,1:T(8,128)}) %reduce-scatter.8.cloned.1.call-update) | async-done | bytes 196624 | tf_op jit(solution)/shard_map/reduce_scatter | solution.py:179
  252.6 13.0 %all_gather.34 = bf16[4,1,16,3072]{3,2,1,0:T(8,128)(2,1)S(1)} all-gather(bf16[1,1,16,3072]{3,2,1,0:T(8,128)(2,1)S(1)} %fusion.171), channel_id=1, replica_groups=mesh['section'=2,'seq'=32,'cfg'=4] {'cfg'}, dimensions={0}, use_global_device_ids=true | all-gather | bytes 491520 | tf_op jit(solution)/shard_map/all_gather | solution.py:65
  265.6 7.1 %convolution_bitcast_fusion.7 = f32[4,8,3,1,16,64]{5,4,1,2,0,3:T(8,128)S(1)} fusion(bf16[3072,3,8,64,1]{0,3,2,1,4:T(8,128)(2,1)} %bitcast.383, bf16[4,1,16,3072]{3,2,1,0:T(8,128)(2,1)S(1)} %all_gather.34), kind=kOutput, calls=%fused_computation.42 | convolution fusion | flops 603979776 | bytes 10223616 | tf_op jit(solution)/shard_map/spqd,djge->sgjpqe/dot_general | solution.py:133
  285.1 10.3 %all-to-all-start.4 = ((bf16[32,3,1,1024]{3,1,2,0:T(4,128)(2,1)}), bf16[32,3,1,1024]{3,1,2,0:T(4,128)(2,1)}, u32[]{:S(2)}, u32[]{:S(2)}) async-start(bf16[32,3,1,1024]{3,1,2,0:T(4,128)(2,1)} %pad_maximum_fusion.2), calls=%async_computation.6 | async-start | bytes 524288 | tf_op jit(solution)/shard_map/all_to_all | solution.py:148
  296.0 9.3 %all-to-all-done.4 = bf16[32,3,1,1024]{3,1,2,0:T(4,128)(2,1)} async-done(((bf16[32,3,1,1024]{3,1,2,0:T(4,128)(2,1)}), bf16[32,3,1,1024]{3,1,2,0:T(4,128)(2,1)}, u32[]{:S(2)}, u32[]{:S(2)}) %all-to-all-start.4) | async-done | bytes 196640 | tf_op jit(solution)/shard_map/all_to_all | solution.py:148
  327.9 14.9 %all_to_all.122 = bf16[32,2,512]{2,1,0:T(2,128)(2,1)} all-to-all(bf16[32,2,512]{2,1,0:T(2,128)(2,1)} %reshape.2912), channel_id=1, replica_groups=mesh['section'=2,'seq'=32,'cfg'=4] {'seq'}, dimensions={0} | all-to-all | bytes 131072 | tf_op jit(solution)/shard_map/all_to_all | solution.py:177
  350.4 19.5 %reduce-scatter.10.cloned.1.call-done = f32[1,1,16,3072]{3,2,0,1:T(8,128)} async-done(((f32[4,1,16,3072]{3,2,0,1:T(8,128)}), f32[1,1,16,3072]{3,2,0,1:T(8,128)}) %reduce-scatter.10.cloned.1.call-update) | async-done | bytes 196624 | tf_op jit(solution)/shard_map/reduce_scatter | solution.py:179
  375.7 13.0 %all_gather.36 = bf16[4,1,16,3072]{3,2,1,0:T(8,128)(2,1)S(1)} all-gather(bf16[1,1,16,3072]{3,2,1,0:T(8,128)(2,1)S(1)} %fusion.172), channel_id=1, replica_groups=mesh['section'=2,'seq'=32,'cfg'=4] {'cfg'}, dimensions={0}, use_global_device_ids=true | all-gather | bytes 491520 | tf_op jit(solution)/shard_map/all_gather | solution.py:65
  408.2 10.2 %all-to-all-start.6 = ((bf16[32,3,1,1024]{3,1,2,0:T(4,128)(2,1)}), bf16[32,3,1,1024]{3,1,2,0:T(4,128)(2,1)}, u32[]{:S(2)}, u32[]{:S(2)}) async-start(bf16[32,3,1,1024]{3,1,2,0:T(4,128)(2,1)} %pad_maximum_fusion.3), calls=%async_computation.9 | async-start | bytes 524288 | tf_op jit(solution)/shard_map/all_to_all | solution.py:148
  419.1 9.2 %all-to-all-done.6 = bf16[32,3,1,1024]{3,1,2,0:T(4,128)(2,1)} async-done(((bf16[32,3,1,1024]{3,1,2,0:T(4,128)(2,1)}), bf16[32,3,1,1024]{3,1,2,0:T(4,128)(2,1)}, u32[]{:S(2)}, u32[]{:S(2)}) %all-to-all-start.6) | async-done | bytes 196640 | tf_op jit(solution)/shard_map/all_to_all | solution.py:148
  450.9 15.1 %all_to_all.123 = bf16[32,2,512]{2,1,0:T(2,128)(2,1)} all-to-all(bf16[32,2,512]{2,1,0:T(2,128)(2,1)} %reshape.2914), channel_id=1, replica_groups=mesh['section'=2,'seq'=32,'cfg'=4] {'seq'}, dimensions={0} | all-to-all | bytes 131072 | tf_op jit(solution)/shard_map/all_to_all | solution.py:177
  473.6 19.4 %reduce-scatter.12.cloned.1.call-done = f32[1,1,16,3072]{3,2,0,1:T(8,128)} async-done(((f32[4,1,16,3072]{3,2,0,1:T(8,128)}), f32[1,1,16,3072]{3,2,0,1:T(8,128)}) %reduce-scatter.12.cloned.1.call-update) | async-done | bytes 196624 | tf_op jit(solution)/shard_map/reduce_scatter | solution.py:179
  498.8 12.9 %all_gather.38 = bf16[4,1,16,3072]{3,2,1,0:T(8,128)(2,1)S(1)} all-gather(bf16[1,1,16,3072]{3,2,1,0:T(8,128)(2,1)S(1)} %fusion.173), channel_id=1, replica_groups=mesh['section'=2,'seq'=32,'cfg'=4] {'cfg'}, dimensions={0}, use_global_device_ids=true | all-gather | bytes 491520 | tf_op jit(solution)/shard_map/all_gather | solution.py:65
  511.7 7.1 %convolution_bitcast_fusion.5 = f32[4,8,3,1,16,64]{5,4,1,2,0,3:T(8,128)S(1)} fusion(bf16[3072,3,8,64,1]{0,3,2,1,4:T(8,128)(2,1)} %bitcast.385, bf16[4,1,16,3072]{3,2,1,0:T(8,128)(2,1)S(1)} %all_gather.38), kind=kOutput, calls=%fused_computation.40 | convolution fusion | flops 603979776 | bytes 10223616 | tf_op jit(solution)/shard_map/spqd,djge->sgjpqe/dot_general | solution.py:133
  531.2 10.2 %all-to-all-start.8 = ((bf16[32,3,1,1024]{3,1,2,0:T(4,128)(2,1)}), bf16[32,3,1,1024]{3,1,2,0:T(4,128)(2,1)}, u32[]{:S(2)}, u32[]{:S(2)}) async-start(bf16[32,3,1,1024]{3,1,2,0:T(4,128)(2,1)} %pad_maximum_fusion.4), calls=%async_computation.12 | async-start | bytes 524288 | tf_op jit(solution)/shard_map/all_to_all | solution.py:148
  542.0 9.3 %all-to-all-done.8 = bf16[32,3,1,1024]{3,1,2,0:T(4,128)(2,1)} async-done(((bf16[32,3,1,1024]{3,1,2,0:T(4,128)(2,1)}), bf16[32,3,1,1024]{3,1,2,0:T(4,128)(2,1)}, u32[]{:S(2)}, u32[]{:S(2)}) %all-to-all-start.8) | async-done | bytes 196640 | tf_op jit(solution)/shard_map/all_to_all | solution.py:148
  602.8 12.9 %reduce-scatter.14.cloned.1.call-done = f32[1,1,16,3072]{3,2,0,1:T(8,128)} async-done(((f32[4,1,16,3072]{3,2,0,1:T(8,128)}), f32[1,1,16,3072]{3,2,0,1:T(8,128)}) %reduce-scatter.14.cloned.1.call-update) | async-done | bytes 196624 | tf_op jit(solution)/shard_map/reduce_scatter | solution.py:179
  619.7 13.0 %all_gather.39 = bf16[4,1,16,3072]{3,2,1,0:T(8,128)(2,1)S(1)} all-gather(bf16[1,1,16,3072]{3,2,1,0:T(8,128)(2,1)S(1)} %get-tuple-element.222), channel_id=1, replica_groups=mesh['section'=2,'seq'=32,'cfg'=4] {'cfg'}, dimensions={0}, use_global_device_ids=true | all-gather | bytes 491520 | tf_op jit(solution)/shard_map/all_gather | solution.py:65
  632.7 12.7 %all_gather.37 = bf16[4,1,16,3072]{3,2,1,0:T(8,128)(2,1)S(1)} all-gather(bf16[1,1,16,3072]{3,2,1,0:T(8,128)(2,1)S(1)} %get-tuple-element.221), channel_id=1, replica_groups=mesh['section'=2,'seq'=32,'cfg'=4] {'cfg'}, dimensions={0}, use_global_device_ids=true | all-gather | bytes 491520 | tf_op jit(solution)/shard_map/all_gather | solution.py:65
  645.9 12.5 %all_gather.35 = bf16[4,1,16,3072]{3,2,1,0:T(8,128)(2,1)S(1)} all-gather(bf16[1,1,16,3072]{3,2,1,0:T(8,128)(2,1)S(1)} %get-tuple-element.220), channel_id=1, replica_groups=mesh['section'=2,'seq'=32,'cfg'=4] {'cfg'}, dimensions={0}, use_global_device_ids=true | all-gather | bytes 491520 | tf_op jit(solution)/shard_map/all_gather | solution.py:65
  658.6 12.5 %all_gather.33 = bf16[4,1,16,3072]{3,2,1,0:T(8,128)(2,1)S(1)} all-gather(bf16[1,1,16,3072]{3,2,1,0:T(8,128)(2,1)S(1)} %get-tuple-element.219), channel_id=1, replica_groups=mesh['section'=2,'seq'=32,'cfg'=4] {'cfg'}, dimensions={0}, use_global_device_ids=true | all-gather | bytes 491520 | tf_op jit(solution)/shard_map/all_gather | solution.py:65
  (334 shorter events, 267.4 us)
Async XLA Ops:
  7.2 638.2 %copy-start = (bf16[3072,64]{0,1:T(8,128)(2,1)S(1)}, bf16[3072,64]{0,1:T(8,128)(2,1)}, u32[]{:S(2)}) copy-start(bf16[3072,64]{0,1:T(8,128)(2,1)} %param.19) | copy-start | bytes 1179652
  7.2 89.2 %all-gather.3.cloned.1.call-start = ((), (), s32[]{:S(2)}) async-start(), calls=%async_computation.20 | async-start | bytes 3244032 | tf_op jit(solution)/shard_map/all_gather | solution.py:96
  10.1 37.5 %copy-start.21 = (pred[16]{0:T(512)(128)(4,1)}, pred[16]{0:T(512)(128)(4,1)S(1)}, u32[]{:S(2)}) copy-start(pred[16]{0:T(512)(128)(4,1)S(1)} %add_compare_fusion.5) | copy-start | bytes 52
  11.5 26.8 %copy-start.7 = (f32[1,1,3072]{2,0,1:T(1,128)}, f32[1,1,3072]{2,0,1:T(1,128)S(1)}, u32[]{:S(2)}) copy-start(f32[1,1,3072]{2,0,1:T(1,128)S(1)} %get-tuple-element.200) | copy-start | bytes 36868
  11.5 26.8 %copy-start.8 = (f32[1,1,3072]{2,0,1:T(1,128)}, f32[1,1,3072]{2,0,1:T(1,128)S(1)}, u32[]{:S(2)}) copy-start(f32[1,1,3072]{2,0,1:T(1,128)S(1)} %get-tuple-element.201) | copy-start | bytes 36868
  11.5 26.8 %copy-start.9 = (f32[1,1,3072]{2,0,1:T(1,128)}, f32[1,1,3072]{2,0,1:T(1,128)S(1)}, u32[]{:S(2)}) copy-start(f32[1,1,3072]{2,0,1:T(1,128)S(1)} %get-tuple-element.203) | copy-start | bytes 36868
  11.5 26.8 %copy-start.10 = (f32[1,1,3072]{2,0,1:T(1,128)}, f32[1,1,3072]{2,0,1:T(1,128)S(1)}, u32[]{:S(2)}) copy-start(f32[1,1,3072]{2,0,1:T(1,128)S(1)} %get-tuple-element.204) | copy-start | bytes 36868
  45.5 17.0 %copy-start.1 = (bf16[1,1,1,2048,128]{4,3,2,1,0:T(8,128)(2,1)S(1)}, bf16[1,1,1,2048,128]{4,3,2,1,0:T(8,128)(2,1)}, u32[]{:S(2)}) copy-start(bf16[1,1,1,2048,128]{4,3,2,1,0:T(8,128)(2,1)} %param.14) | copy-start | bytes 1572868
  45.5 17.1 %copy-start.26 = (s32[2]{0:T(128)S(1)}, s32[2]{0:T(128)}, u32[]{:S(2)}) copy-start(s32[2]{0:T(128)} %param.21) | copy-start | bytes 28
  45.5 17.7 %copy-start.27 = (s32[4]{0:T(128)S(1)}, s32[4]{0:T(128)}, u32[]{:S(2)}) copy-start(s32[4]{0:T(128)} %param.22) | copy-start | bytes 52
  50.8 24.0 %all-to-all-start = ((bf16[32,3,1,1024]{3,1,2,0:T(4,128)(2,1)}), bf16[32,3,1,1024]{3,1,2,0:T(4,128)(2,1)S(1)}, u32[]{:S(2)}, u32[]{:S(2)}) async-start(bf16[32,3,1,1024]{3,1,2,0:T(4,128)(2,1)} %pad_maximum_fusion), calls=%async_computation | async-start | bytes 524288 | tf_op jit(solution)/shard_map/all_to_all | solution.py:148
  62.4 60.7 %reduce-scatter.6.cloned.1.call-start = ((), (), s32[]{:S(2)}) async-start(), calls=%async_computation.15 | async-start | bytes 983040 | tf_op jit(solution)/shard_map/reduce_scatter | solution.py:179
  124.2 1.7 collective-permute-start
  160.6 20.1 %all-to-all-start.2 = ((bf16[32,3,1,1024]{3,1,2,0:T(4,128)(2,1)}), bf16[32,3,1,1024]{3,1,2,0:T(4,128)(2,1)}, u32[]{:S(2)}, u32[]{:S(2)}) async-start(bf16[32,3,1,1024]{3,1,2,0:T(4,128)(2,1)} %pad_maximum_fusion.1), calls=%async_computation.3 | async-start | bytes 524288 | tf_op jit(solution)/shard_map/all_to_all | solution.py:148
  170.8 75.0 %reduce-scatter.8.cloned.1.call-start = ((), (), s32[]{:S(2)}) async-start(), calls=%async_computation.16 | async-start | bytes 983040 | tf_op jit(solution)/shard_map/reduce_scatter | solution.py:179
  247.6 1.6 collective-permute-start.1
  265.6 8.9 %copy-start.14 = (f32[2,16,32]{2,1,0:T(8,128)S(1)}, f32[2,16,32]{2,1,0:T(8,128)}, u32[]{:S(2)}) copy-start(f32[2,16,32]{2,1,0:T(8,128)} %get-tuple-element.258) | copy-start | bytes 12292
  265.6 8.9 %copy-start.13 = (f32[2,16,32]{2,1,0:T(8,128)S(1)}, f32[2,16,32]{2,1,0:T(8,128)}, u32[]{:S(2)}) copy-start(f32[2,16,32]{2,1,0:T(8,128)} %get-tuple-element.257) | copy-start | bytes 12292
  285.1 20.2 %all-to-all-start.4 = ((bf16[32,3,1,1024]{3,1,2,0:T(4,128)(2,1)}), bf16[32,3,1,1024]{3,1,2,0:T(4,128)(2,1)}, u32[]{:S(2)}, u32[]{:S(2)}) async-start(bf16[32,3,1,1024]{3,1,2,0:T(4,128)(2,1)} %pad_maximum_fusion.2), calls=%async_computation.6 | async-start | bytes 524288 | tf_op jit(solution)/shard_map/all_to_all | solution.py:148
  295.4 74.4 %reduce-scatter.10.cloned.1.call-start = ((), (), s32[]{:S(2)}) async-start(), calls=%async_computation.17 | async-start | bytes 983040 | tf_op jit(solution)/shard_map/reduce_scatter | solution.py:179
  370.9 1.4 collective-permute-start.2
  388.7 8.9 %copy-start.15 = (f32[2,16,32]{2,1,0:T(8,128)S(1)}, f32[2,16,32]{2,1,0:T(8,128)}, u32[]{:S(2)}) copy-start(f32[2,16,32]{2,1,0:T(8,128)} %get-tuple-element.233) | copy-start | bytes 12292
  408.2 20.1 %all-to-all-start.6 = ((bf16[32,3,1,1024]{3,1,2,0:T(4,128)(2,1)}), bf16[32,3,1,1024]{3,1,2,0:T(4,128)(2,1)}, u32[]{:S(2)}, u32[]{:S(2)}) async-start(bf16[32,3,1,1024]{3,1,2,0:T(4,128)(2,1)} %pad_maximum_fusion.3), calls=%async_computation.9 | async-start | bytes 524288 | tf_op jit(solution)/shard_map/all_to_all | solution.py:148
  418.4 74.5 %reduce-scatter.12.cloned.1.call-start = ((), (), s32[]{:S(2)}) async-start(), calls=%async_computation.18 | async-start | bytes 983040 | tf_op jit(solution)/shard_map/reduce_scatter | solution.py:179
  494.1 1.4 collective-permute-start.3
  511.7 8.9 %copy-start.11 = (f32[2,16,32]{2,1,0:T(8,128)S(1)}, f32[2,16,32]{2,1,0:T(8,128)}, u32[]{:S(2)}) copy-start(f32[2,16,32]{2,1,0:T(8,128)} %get-tuple-element.231) | copy-start | bytes 12292
  531.2 20.1 %all-to-all-start.8 = ((bf16[32,3,1,1024]{3,1,2,0:T(4,128)(2,1)}), bf16[32,3,1,1024]{3,1,2,0:T(4,128)(2,1)}, u32[]{:S(2)}, u32[]{:S(2)}) async-start(bf16[32,3,1,1024]{3,1,2,0:T(4,128)(2,1)} %pad_maximum_fusion.4), calls=%async_computation.12 | async-start | bytes 524288 | tf_op jit(solution)/shard_map/all_to_all | solution.py:148
  566.6 49.0 %copy-start.19 = (pred[16]{0:T(512)(128)(4,1)S(1)}, pred[16]{0:T(512)(128)(4,1)}, u32[]{:S(2)}) copy-start(pred[16]{0:T(512)(128)(4,1)} %get-tuple-element.284) | copy-start | bytes 52
  573.9 14.8 %all-to-all-start.9 = ((bf16[32,2,512]{2,1,0:T(2,128)(2,1)}), bf16[32,2,512]{2,1,0:T(2,128)(2,1)}, u32[]{:S(2)}, u32[]{:S(2)}) async-start(bf16[32,2,512]{2,1,0:T(2,128)(2,1)} %reshape.2916), calls=%async_computation.13 | async-start | bytes 131072 | tf_op jit(solution)/shard_map/all_to_all | solution.py:177
  579.9 35.7 %reduce-scatter.14.cloned.1.call-start = ((), (), s32[]{:S(2)}) async-start(), calls=%async_computation.19 | async-start | bytes 983040 | tf_op jit(solution)/shard_map/reduce_scatter | solution.py:179
  596.2 75.2 %copy-start.17 = (f32[1,4,16,64]{3,2,1,0:T(8,128)S(1)}, f32[1,4,16,64]{3,2,1,0:T(8,128)}, u32[]{:S(2)}) copy-start(f32[1,4,16,64]{3,2,1,0:T(8,128)} %param.13) | copy-start | bytes 49156
  616.7 1.4 collective-permute-start.4
  (13 other events, 45.7 us)
Sparse Core Ops, SparseCore 0:
  10.6 82.7 all-gather.2
  102.2 20.8 reduce-scatter.5
  226.7 19.1 reduce-scatter.7
  350.5 19.3 reduce-scatter.9
  473.7 19.2 reduce-scatter.11
  596.3 19.2 reduce-scatter.13
where the time goes:
time: 693 us; the launch traced here: 681 us
  blocking collectives  175 us (25%)
  waiting for transfers between devices  150 us (22%)
  local copies, waits for them, and re-layouts  118 us (17%)
  other arithmetic  98.2 us (14%)
  matrix products  64.8 us (9%)
  starting transfers between devices  59.3 us (9%)
  between operations  15.7 us (2%)
    all_gather x9, blocking collectives, spread(): return lax.all_gather(values, 'cfg', axis=0, tiled=True)  116 us
    reduce_scatter x5, waiting for transfers between devices, per_device(): lax.psum_scatter(jnp.einsum('sgpqe,dge->spqd', returned, out_full, prefer...  89.6 us
    all_to_all x4, blocking collectives, per_device(): lax.all_to_all(attended, 'seq', split_axis=2, concat_axis=0, tiled=True)  59.5 us
    all_to_all x5, starting transfers between devices, per_device(): lax.all_to_all(outgoing, 'seq', split_axis=0, concat_axis=3, tiled=True)  52.4 us
    all_to_all x5, waiting for transfers between devices, per_device(): lax.all_to_all(outgoing, 'seq', split_axis=0, concat_axis=3, tiled=True)  46.8 us
    dot_general x5, matrix products, per_device(): jnp.einsum('spqd,djge->sgjpqe', mixed_rows, qkv_full, preferred_element_t...  35.5 us
    unnamed x69, local copies, waits for them, and re-layouts  25.6 us
    another operation x15, local copies, waits for them, and re-layouts, per_device(): jnp.stack([queries, key_part, projected[:, :, 2]], axis=2)  20.4 us
  transfers between devices with their start and end apart: 17, of which 15 were waited for; matrix products, arithmetic and copies ran while one was open for 8% of the time, Pallas kernels for 0%

commit v1 on v0

v1 whole, which is shorter than its diff:
```python
import math

import jax
import jax.numpy as jnp
from jax import lax
from jax.sharding import PartitionSpec as P

HD = 64
TEXT = 226


def from_behind(value, axis, steps):
    count = lax.axis_size(axis)
    pairs = [(source, (source + steps) % count) for source in range(count)]
    return lax.ppermute(value, axis, pairs)


def row_norm(values):
    centered = values - jnp.mean(values, axis=-1, keepdims=True)
    return centered * lax.rsqrt(jnp.mean(centered * centered, axis=-1, keepdims=True) + 1e-05)


def head_norm(values):
    centered = values - jnp.mean(values, axis=-1, keepdims=True)
    return centered * lax.rsqrt(jnp.mean(centered * centered, axis=-1, keepdims=True) + 1e-06)


def rope_angles(places, head_size):
    half_size = head_size // 2
    pairs_t = head_size // 8
    pairs_h = (half_size - pairs_t) // 2
    pair_index = jnp.arange(half_size)
    first_part = pair_index < pairs_t
    second_part = jnp.logical_and(pair_index >= pairs_t, pair_index < pairs_t + pairs_h)
    third_part = pair_index >= pairs_t + pairs_h
    local_index = jnp.where(
        first_part,
        pair_index,
        jnp.where(second_part, pair_index - pairs_t, pair_index - pairs_t - pairs_h),
    )
    axis_span = jnp.where(first_part, 2 * pairs_t, 2 * pairs_h)
    frequency = jnp.exp(
        -math.log(10000.0) * 2.0 * local_index.astype(jnp.float32) / axis_span.astype(jnp.float32)
    )
    angles = places[0][..., None] * first_part.astype(jnp.float32)
    angles = angles + places[1][..., None] * second_part.astype(jnp.float32)
    angles = angles + places[2][..., None] * third_part.astype(jnp.float32)
    return angles * frequency


def rotate(values, cos_table, sin_table):
    half_size = values.shape[-1] // 2
    first_half = values[..., :half_size]
    second_half = values[..., half_size:]
    return jnp.concatenate(
        [
            first_half * cos_table - second_half * sin_table,
            second_half * cos_table + first_half * sin_table,
        ],
        axis=-1,
    )


def per_device(
    hidden_states,
    latent,
    stale_cache,
    qkv_weight,
    out_weight,
    modulation,
    out_modulation,
    proj_weight,
    solver_coef,
    video_len,
    text_len,
    positions,
):
    section_id = lax.axis_index("section")
    shard_id = lax.axis_index("seq")
    seq_devices = lax.axis_size("seq")
    cfg_devices = lax.axis_size("cfg")
    patches = hidden_states.shape[1]
    patch_dev = hidden_states.shape[2]
    width = hidden_states.shape[3]
    patch_len = patch_dev * seq_devices
    total_len = patch_len * patches
    group_heads = qkv_weight.shape[3] // HD
    seq_count = cfg_devices
    qkv_full = qkv_weight[0].reshape(width, 3, group_heads, HD)
    out_full = lax.all_gather(out_weight[0], "seq", axis=0, tiled=True).reshape(
        width, group_heads, HD
    )
    mod_rows = modulation[0]
    stale_rows = stale_cache[0, 0, 0]
    my_sequence = shard_id // group_heads
    row_ids = jnp.arange(total_len)
    text_limit = lax.dynamic_index_in_dim(text_len, my_sequence, keepdims=False)
    video_limit = lax.dynamic_index_in_dim(video_len, my_sequence // 2, keepdims=False)
    live_keys = jnp.where(row_ids < TEXT, row_ids < text_limit, row_ids - TEXT < video_limit)
    key_patch = row_ids // patch_len
    use_fresh = key_patch[None, :] <= jnp.arange(patches)[:, None]
    scale_factor = HD ** (-0.5)

    row_place = (
        jnp.arange(patches)[:, None] * patch_len
        + shard_id * patch_dev
        + jnp.arange(patch_dev)[None, :]
    )
    text_rows = (row_place < TEXT)[:, :, None]
    shift_rows = jnp.where(text_rows, mod_rows[3], mod_rows[0])
    scale_rows = jnp.where(text_rows, mod_rows[4], mod_rows[1])
    gate_rows = jnp.where(text_rows, mod_rows[5], mod_rows[2])
    angles = rope_angles(positions.astype(jnp.float32), HD)
    angles = jnp.where(text_rows[None], 0.0, angles)
    angles = jnp.repeat(angles, 2, axis=0)[:, None]
    cos_table = jnp.cos(angles)
    sin_table = jnp.sin(angles)

    def run(hidden):
        normed = row_norm(hidden.astype(jnp.float32))
        mixed_rows = (normed * (1.0 + scale_rows) + shift_rows).astype(jnp.bfloat16)
        mixed_rows = lax.all_gather(mixed_rows, "cfg", axis=0, tiled=True)
        projected = jnp.einsum(
            "spqd,djge->sgjpqe", mixed_rows, qkv_full, preferred_element_type=jnp.float32
        )
        queries = rotate(head_norm(projected[:, :, 0]), cos_table, sin_table)
        key_part = rotate(head_norm(projected[:, :, 1]), cos_table, sin_table)
        stacked = jnp.stack([queries, key_part, projected[:, :, 2]], axis=2).astype(jnp.bfloat16)
        outgoing = stacked.reshape(seq_count * group_heads, 3, patches, patch_dev * HD)
        incoming = lax.all_to_all(outgoing, "seq", split_axis=0, concat_axis=3, tiled=True)
        incoming = incoming.reshape(3, patches, patch_len, HD)
        fresh_rows = jnp.concatenate([incoming[1], incoming[2]], axis=-1).reshape(
            total_len, 2 * HD
        )
        key_rows = jnp.where(use_fresh[:, :, None], fresh_rows[None], stale_rows[None])
        scores = (
            jnp.einsum(
                "pqe,pke->pqk", incoming[0], key_rows[..., :HD], preferred_element_type=jnp.float32
            )
            * scale_factor
        )
        scores = jnp.where(live_keys[None, None, :], scores, -jnp.inf)
        row_max = jnp.max(scores, axis=-1, keepdims=True)
        weights = jnp.exp(scores - row_max)
        row_sum = jnp.sum(weights, axis=-1, keepdims=True)
        combined = jnp.einsum(
            "pqk,pke->pqe",
            weights.astype(jnp.bfloat16),
            key_rows[..., HD:],
            preferred_element_type=jnp.float32,
        )
        attended = (combined / row_sum).astype(jnp.bfloat16)
        attended = attended.reshape(patches, seq_devices, patch_dev * HD)[None]
        returned = lax.all_to_all(attended, "seq", split_axis=2, concat_axis=0, tiled=True)
        returned = returned.reshape(seq_count, group_heads, patches, patch_dev, HD)
        update = lax.psum_scatter(
            jnp.einsum("sgpqe,dge->spqd", returned, out_full, preferred_element_type=jnp.float32),
            "cfg",
            scatter_dimension=0,
            tiled=True,
        )
        result = (hidden.astype(jnp.float32) + gate_rows * update).astype(jnp.bfloat16)
        return result, fresh_rows

    first_out, first_cache = run(hidden_states)
    received = from_behind(first_out, "section", 1)
    second_out, second_cache = run(received)
    key_cache = jnp.where(section_id == 0, first_cache, second_cache)

    normed = row_norm(second_out.astype(jnp.float32))
    normed_out = (normed * (1.0 + out_modulation[1]) + out_modulation[0]).astype(jnp.bfloat16)
    predicted = jnp.einsum(
        "spqd,do->spqo", normed_out, proj_weight, preferred_element_type=jnp.float32
    )
    predicted_all = lax.all_gather(predicted, ("section", "cfg"), axis=0, tiled=True)
    predicted_all = predicted_all[predicted_all.shape[0] - seq_count :]
    pair_rows = lax.dynamic_slice_in_dim(predicted_all, 2 * section_id, 2, 0)
    solver_row = solver_coef[0]
    guided = pair_rows[0] + solver_row[2] * (pair_rows[1] - pair_rows[0])
    new_latent = solver_row[0] * latent[0] + solver_row[1] * guided
    return (new_latent[None], key_cache[None, None, None])


def solution(mesh):
    return jax.shard_map(
        per_device,
        mesh=mesh,
        in_specs=(
            P("cfg", None, "seq", None),
            P("section", None, "seq", None),
            P("section", "cfg", "seq", None, None),
            P("section", None, None, "cfg"),
            P("section", "seq", "cfg"),
            P("section", None, None),
            P(),
            P(),
            P("section", None),
            P(),
            P(),
            P(None, None, None, "seq"),
        ),
        out_specs=(P("section", None, "seq", None), P("section", "cfg", "seq", None, None)),
        check_vma=False,
    )
```

time: 693 us -> 405 us (0.58)
  the two profiles are of different devices: /device:TPU:2 before, /device:TPU:1 now
where the time goes in v1:
time: 405 us; the launch traced here: 397 us
  waiting for transfers between devices  170 us (42%)
  blocking collectives  84.7 us (21%)
  local copies, waits for them, and re-layouts  39.7 us (10%)
  matrix products  39.5 us (10%)
  other arithmetic  35.8 us (9%)
  between operations  16.7 us (4%)
  starting transfers between devices  10.8 us (3%)
    reduce_scatter x2, waiting for transfers between devices, run(): lax.psum_scatter(jnp.einsum('sgpqe,dge->spqd', returned, out_full, prefer...  75.6 us
    all_gather x2, waiting for transfers between devices, run(): mixed_rows = lax.all_gather(mixed_rows, 'cfg', axis=0, tiled=True)  48.3 us
    all_to_all x2, blocking collectives, run(): lax.all_to_all(attended, 'seq', split_axis=2, concat_axis=0, tiled=True)  32 us
    all_to_all x1, blocking collectives, run(): lax.all_to_all(outgoing, 'seq', split_axis=0, concat_axis=3, tiled=True)  30.7 us
    all_gather x1, waiting for transfers between devices, per_device(): lax.all_gather(out_weight[0], 'seq', axis=0, tiled=True)  27.8 us
    all_gather x1, blocking collectives, per_device(): lax.all_gather(predicted, ('section', 'cfg'), axis=0, tiled=True)  22.1 us
    dot_general x2, matrix products, run(): jnp.einsum('spqd,djge->sgjpqe', mixed_rows, qkv_full, preferred_element_t...  16.2 us
    all_to_all x1, waiting for transfers between devices, run(): lax.all_to_all(outgoing, 'seq', split_axis=0, concat_axis=3, tiled=True)  15.9 us
  transfers between devices with their start and end apart: 7, of which 7 were waited for; matrix products, arithmetic and copies ran while one was open for 9% of the time, Pallas kernels for 0%

profile of v1, /device:TPU:1, one launch (start us, length us, event | category | flops | bytes accessed | tf_op | source)
XLA Modules:
  0.0 396.7 jit_solution(5097558336061669999)
XLA Ops:
  8.2 1.4 fusion.91
  12.0 2.0 fusion.58
  14.1 12.7 %copy.39 = bf16[1,3072,3,512]{1,3,2,0:T(8,128)(2,1)} copy(bf16[1,3072,3,512]{3,1,2,0:T(8,128)(2,1)} %param.15) | data formatting | bytes 18874368 | tf_op args[3]
  27.2 19.9 %all-gather.6.cloned.1.call-done = bf16[4,4,16,3072]{3,2,1,0:T(8,128)(2,1)} async-done(((bf16[1,4,16,3072]{3,2,1,0:T(8,128)(2,1)}), bf16[4,4,16,3072]{3,2,1,0:T(8,128)(2,1)}) %all-gather.6.cloned.1.call-update) | async-done | bytes 1572880 | tf_op jit(solution)/shard_map/all_gather | solution.py:122
  47.1 8.1 %convolution_bitcast_fusion.3 = f32[4,8,3,4,16,64]{5,4,1,2,3,0:T(8,128)S(1)} fusion(bf16[3072,3,8,64,1,1]{0,3,2,1,5,4:T(8,128)(2,1)} %bitcast.167, bf16[4,4,16,3072]{3,2,1,0:T(8,128)(2,1)} %all-gather.6.cloned.1.call-done), kind=kOutput, calls=%fused_computation.19 | convolution fusion | flops 2415919104 | bytes 12582912 | tf_op jit(solution)/shard_map/spqd,djge->sgjpqe/dot_general | solution.py:123
  56.1 1.3 multiply_reduce_fusion.3
  61.4 1.5 copy.44
  62.9 9.5 %all-to-all-start = ((bf16[32,3,4,1024]{3,2,1,0:T(4,128)(2,1)}), bf16[32,3,4,1024]{3,2,1,0:T(4,128)(2,1)S(1)}, u32[]{:S(2)}, u32[]{:S(2)}) async-start(bf16[32,3,4,1024]{3,2,1,0:T(4,128)(2,1)} %copy.44), calls=%async_computation | async-start | bytes 1572864 | tf_op jit(solution)/shard_map/all_to_all | solution.py:130
  77.6 15.9 %all-to-all-done = bf16[32,3,4,1024]{3,2,1,0:T(4,128)(2,1)S(1)} async-done(((bf16[32,3,4,1024]{3,2,1,0:T(4,128)(2,1)}), bf16[32,3,4,1024]{3,2,1,0:T(4,128)(2,1)S(1)}, u32[]{:S(2)}, u32[]{:S(2)}) %all-to-all-start) | async-done | bytes 786464 | tf_op jit(solution)/shard_map/all_to_all | solution.py:130
  96.6 2.5 fusion
  99.2 3.7 fusion.2
  102.9 4.0 %fusion.25 = bf16[4,512,64]{1,2,0:T(8,128)(2,1)S(1)} fusion(bf16[4,2048,128]{1,2,0:T(8,128)(2,1)S(1)} %broadcast_select_fusion.1, f32[4,512,2048]{2,1,0:T(8,128)S(1)} %get-tuple-element.49, f32[4,512]{1,0:T(4,128)S(1)} %get-tuple-element.48, pred[2048]{0:T(1024)(128)(4,1)S(1)} %fusion.78, f32[4,512]{1,0:T(4,128)S(1)} %fusion.2), kind=kOutput, calls=%fused_computation.58 | convolution fusion | flops 553910272 | bytes 18106368 | tf_op jit(solution)/shard_map/pqk,pke->pqe/dot_general | solution.py:146
  107.8 16.1 %all_to_all.60 = bf16[1,4,32,1024]{3,1,0,2:T(4,128)(2,1)S(1)} all-to-all(bf16[1,4,32,1024]{3,1,0,2:T(4,128)(2,1)S(1)} %copy.52), channel_id=1, replica_groups=mesh['section'=2,'seq'=32,'cfg'=4] {'seq'}, dimensions={2} | all-to-all | bytes 524288 | tf_op jit(solution)/shard_map/all_to_all | solution.py:154
  124.3 27.8 %all-gather.10.cloned.1.call-done = bf16[1,3072,512]{2,1,0:T(8,128)(2,1)} async-done(((bf16[1,96,512]{2,1,0:T(8,128)(2,1)}), bf16[1,3072,512]{2,1,0:T(8,128)(2,1)}) %all-gather.10.cloned.1.call-update) | async-done | bytes 3145744 | tf_op jit(solution)/shard_map/all_gather | solution.py:90
  152.0 4.6 %copy.54 = bf16[1,3072,512]{1,2,0:T(8,128)(2,1)} copy(bf16[1,3072,512]{2,1,0:T(8,128)(2,1)} %all-gather.10.cloned.1.call-done) | data formatting | bytes 6291456 | tf_op jit(solution)/shard_map/all_gather | solution.py:90
  156.7 4.5 %convolution_bitcast_fusion.1 = f32[4,4,16,3072]{3,2,1,0:T(8,128)} fusion(bf16[4,8,4,16,64]{4,3,2,1,0:T(8,128)(2,1)S(1)} %reshape.453, bf16[3072,8,64,1,1]{0,2,4,1,3:T(8,128)(2,1)} %bitcast.169), kind=kOutput, calls=%fused_computation.15 | convolution fusion | flops 805306368 | bytes 6553600 | tf_op jit(solution)/shard_map/sgpqe,dge->spqd/dot_general | solution.py:157
  161.3 41.5 %reduce-scatter.3.cloned.1.call-done = f32[1,4,16,3072]{3,2,1,0:T(8,128)} async-done(((f32[4,4,16,3072]{3,2,1,0:T(8,128)}), f32[1,4,16,3072]{3,2,1,0:T(8,128)}) %reduce-scatter.3.cloned.1.call-update) | async-done | bytes 786448 | tf_op jit(solution)/shard_map/reduce_scatter | solution.py:156
  204.9 1.3 collective-permute-done
  208.0 28.4 %all-gather.8.cloned.1.call-done = bf16[4,4,16,3072]{3,2,1,0:T(8,128)(2,1)} async-done(((bf16[1,4,16,3072]{3,2,1,0:T(8,128)(2,1)}), bf16[4,4,16,3072]{3,2,1,0:T(8,128)(2,1)}) %all-gather.8.cloned.1.call-update) | async-done | bytes 1572880 | tf_op jit(solution)/shard_map/all_gather | solution.py:122
  236.4 8.1 %convolution_bitcast_fusion.2 = f32[4,8,3,4,16,64]{5,4,1,3,0,2:T(8,128)S(1)} fusion(bf16[3072,3,8,64,1,1]{0,3,2,5,4,1:T(8,128)(2,1)} %bitcast.168, bf16[4,4,16,3072]{3,2,1,0:T(8,128)(2,1)} %all-gather.8.cloned.1.call-done), kind=kOutput, calls=%fused_computation.18 | convolution fusion | flops 2415919104 | bytes 12582912 | tf_op jit(solution)/shard_map/spqd,djge->sgjpqe/dot_general | solution.py:123
  252.9 30.7 %all_to_all.61 = bf16[32,3,4,1024]{3,2,1,0:T(4,128)(2,1)S(1)} all-to-all(bf16[32,3,4,1024]{3,2,1,0:T(4,128)(2,1)S(1)} %copy.60), channel_id=1, replica_groups=mesh['section'=2,'seq'=32,'cfg'=4] {'seq'}, dimensions={0} | all-to-all | bytes 1572864 | tf_op jit(solution)/shard_map/all_to_all | solution.py:130
  288.0 1.7 copy.61
  291.1 2.5 fusion.1
  293.6 3.7 fusion.4
  297.4 4.7 %fusion.35 = bf16[4,512,64]{1,2,0:T(8,128)(2,1)} fusion(bf16[4,2048,128]{1,2,0:T(8,128)(2,1)S(1)} %broadcast_select_fusion, f32[4,512,2048]{2,1,0:T(8,128)S(1)} %get-tuple-element.51, f32[4,512]{1,0:T(4,128)S(1)} %get-tuple-element.50, pred[2048]{0:T(1024)(128)(4,1)S(1)} %fusion.78, f32[4,512]{1,0:T(4,128)S(1)} %fusion.4), kind=kOutput, calls=%fused_computation.60 | convolution fusion | flops 553910272 | bytes 18106368 | tf_op jit(solution)/shard_map/pqk,pke->pqe/dot_general | solution.py:146
  303.9 16.0 %all_to_all.62 = bf16[1,4,32,1024]{3,1,0,2:T(4,128)(2,1)S(1)} all-to-all(bf16[1,4,32,1024]{3,1,0,2:T(4,128)(2,1)S(1)} %copy.67), channel_id=1, replica_groups=mesh['section'=2,'seq'=32,'cfg'=4] {'seq'}, dimensions={2} | all-to-all | bytes 524288 | tf_op jit(solution)/shard_map/all_to_all | solution.py:154
  320.3 4.6 %convolution_bitcast_fusion = f32[4,4,16,3072]{3,2,1,0:T(8,128)} fusion(bf16[4,8,4,16,64]{4,3,2,1,0:T(8,128)(2,1)S(1)} %reshape.454, bf16[3072,8,64,1,1]{0,2,4,1,3:T(8,128)(2,1)} %bitcast.170), kind=kOutput, calls=%fused_computation.14 | convolution fusion | flops 805306368 | bytes 6553600 | tf_op jit(solution)/shard_map/sgpqe,dge->spqd/dot_general | solution.py:157
  327.0 1.4 maximum_select_fusion
  328.4 34.1 %reduce-scatter.5.cloned.1.call-done = f32[1,4,16,3072]{3,2,1,0:T(8,128)} async-done(((f32[4,4,16,3072]{3,2,1,0:T(8,128)}), f32[1,4,16,3072]{3,2,1,0:T(8,128)}) %reduce-scatter.5.cloned.1.call-update) | async-done | bytes 786448 | tf_op jit(solution)/shard_map/reduce_scatter | solution.py:156
  362.4 1.4 convert_reduce_fusion.2
  364.5 22.1 %all-gather.1 = f32[32,16,64]{2,1,0:T(8,128)S(1)} all-gather(f32[4,16,64]{2,1,0:T(8,128)S(1)} %fusion.63), channel_id=3, replica_groups=mesh['section'=2,'seq'=32,'cfg'=4] {'section','cfg'}, dimensions={0}, use_global_device_ids=true | all-gather | bytes 147456 | tf_op jit(solution)/shard_map/all_gather | solution.py:175
  386.6 2.5 fusion.75
  (167 shorter events, 39.6 us)
Async XLA Ops:
  8.0 356.1 %copy-start = (bf16[3072,64]{0,1:T(8,128)(2,1)S(1)}, bf16[3072,64]{0,1:T(8,128)(2,1)}, u32[]{:S(2)}) copy-start(bf16[3072,64]{0,1:T(8,128)(2,1)} %param.19) | copy-start | bytes 1179652
  8.0 39.1 %all-gather.6.cloned.1.call-start = ((), (), s32[]{:S(2)}) async-start(), calls=%async_computation.6 | async-start | bytes 1966080 | tf_op jit(solution)/shard_map/all_gather | solution.py:122
  8.1 18.7 %copy-start.22 = (pred[4,16]{1,0:T(4,128)(4,1)}, pred[4,16]{1,0:T(4,128)(4,1)S(1)}, u32[]{:S(2)}) copy-start(pred[4,16]{1,0:T(4,128)(4,1)S(1)} %add_compare_fusion.1) | copy-start | bytes 196
  9.5 2.4 copy-start.11
  9.6 2.4 copy-start.13
  9.6 2.4 copy-start.15
  9.6 2.4 copy-start.17
  14.1 12.7 %copy-start.24 = (s32[3,2,4,16]{3,2,1,0:T(4,128)S(1)}, s32[3,2,4,16]{3,2,1,0:T(4,128)}, u32[]{:S(2)}) copy-start(s32[3,2,4,16]{3,2,1,0:T(4,128)} %param.23) | copy-start | bytes 4612
  59.5 15.0 %copy-start.26 = (s32[2]{0:T(128)S(1)}, s32[2]{0:T(128)}, u32[]{:S(2)}) copy-start(s32[2]{0:T(128)} %param.21) | copy-start | bytes 28
  59.5 15.6 %copy-start.27 = (s32[4]{0:T(128)S(1)}, s32[4]{0:T(128)}, u32[]{:S(2)}) copy-start(s32[4]{0:T(128)} %param.22) | copy-start | bytes 52
  62.9 30.6 %all-to-all-start = ((bf16[32,3,4,1024]{3,2,1,0:T(4,128)(2,1)}), bf16[32,3,4,1024]{3,2,1,0:T(4,128)(2,1)S(1)}, u32[]{:S(2)}, u32[]{:S(2)}) async-start(bf16[32,3,4,1024]{3,2,1,0:T(4,128)(2,1)} %copy.44), calls=%async_computation | async-start | bytes 1572864 | tf_op jit(solution)/shard_map/all_to_all | solution.py:130
  72.4 79.6 %all-gather.10.cloned.1.call-start = ((), (), s32[]{:S(2)}) async-start(), calls=%async_computation.10 | async-start | bytes 3244032 | tf_op jit(solution)/shard_map/all_gather | solution.py:90
  73.0 129.8 %reduce-scatter.3.cloned.1.call-start = ((), (), s32[]{:S(2)}) async-start(), calls=%async_computation.7 | async-start | bytes 3932160 | tf_op jit(solution)/shard_map/reduce_scatter | solution.py:156
  93.9 1.3 copy-start.2
  124.2 78.7 %copy-start.1 = (bf16[1,4,16,3072]{3,2,1,0:T(8,128)(2,1)S(1)}, bf16[1,4,16,3072]{3,2,1,0:T(8,128)(2,1)}, u32[]{:S(2)}) copy-start(bf16[1,4,16,3072]{3,2,1,0:T(8,128)(2,1)} %param.12) | copy-start | bytes 1179652
  124.2 78.6 %copy-start.10 = (f32[1,1,3072]{2,0,1:T(1,128)S(1)}, f32[1,1,3072]{2,0,1:T(1,128)}, u32[]{:S(2)}) copy-start(f32[1,1,3072]{2,0,1:T(1,128)} %get-tuple-element.35) | copy-start | bytes 36868
  124.2 78.6 %copy-start.23 = (pred[4,16]{1,0:T(4,128)(4,1)S(1)}, pred[4,16]{1,0:T(4,128)(4,1)}, u32[]{:S(2)}) copy-start(pred[4,16]{1,0:T(4,128)(4,1)} %copy-done.22) | copy-start | bytes 196
  124.2 82.4 %copy-start.12 = (f32[1,1,3072]{2,0,1:T(1,128)S(1)}, f32[1,1,3072]{2,0,1:T(1,128)}, u32[]{:S(2)}) copy-start(f32[1,1,3072]{2,0,1:T(1,128)} %copy-done.11) | copy-start | bytes 36868
  124.2 82.4 %copy-start.14 = (f32[1,1,3072]{2,0,1:T(1,128)S(1)}, f32[1,1,3072]{2,0,1:T(1,128)}, u32[]{:S(2)}) copy-start(f32[1,1,3072]{2,0,1:T(1,128)} %copy-done.13) | copy-start | bytes 36868
  124.2 82.4 %copy-start.16 = (f32[1,1,3072]{2,0,1:T(1,128)S(1)}, f32[1,1,3072]{2,0,1:T(1,128)}, u32[]{:S(2)}) copy-start(f32[1,1,3072]{2,0,1:T(1,128)} %copy-done.15) | copy-start | bytes 36868
  124.2 82.4 %copy-start.18 = (f32[1,1,3072]{2,0,1:T(1,128)S(1)}, f32[1,1,3072]{2,0,1:T(1,128)}, u32[]{:S(2)}) copy-start(f32[1,1,3072]{2,0,1:T(1,128)} %copy-done.17) | copy-start | bytes 36868
  161.2 75.2 %all-gather.8.cloned.1.call-start = ((), (), s32[]{:S(2)}) async-start(), calls=%async_computation.8 | async-start | bytes 1966080 | tf_op jit(solution)/shard_map/all_gather | solution.py:122
  204.2 2.1 collective-permute-start
  207.7 154.7 %reduce-scatter.5.cloned.1.call-start = ((), (), s32[]{:S(2)}) async-start(), calls=%async_computation.9 | async-start | bytes 3932160 | tf_op jit(solution)/shard_map/reduce_scatter | solution.py:156
  250.1 36.6 %copy-start.19 = (pred[4,2048]{1,0:T(4,128)(4,1)S(1)}, pred[4,2048]{1,0:T(4,128)(4,1)}, u32[]{:S(2)}) copy-start(pred[4,2048]{1,0:T(4,128)(4,1)} %iota_compare_fusion) | copy-start | bytes 24580
  302.0 22.9 %copy-start.25 = (f32[1,3]{1,0:T(1,128)S(1)}, f32[1,3]{1,0:T(1,128)}, u32[]{:S(2)}) copy-start(f32[1,3]{1,0:T(1,128)} %param.20) | copy-start | bytes 40
  302.0 23.5 %copy-start.21 = (f32[2,3072]{1,0:T(2,128)S(1)}, f32[2,3072]{1,0:T(2,128)}, u32[]{:S(2)}) copy-start(f32[2,3072]{1,0:T(2,128)} %param.18) | copy-start | bytes 73732
  302.0 23.5 %copy-start.3 = (bf16[1,1,4,32,1024]{4,3,2,1,0:T(8,128)(2,1)S(1)}, bf16[1,1,4,32,1024]{4,3,2,1,0:T(8,128)(2,1)}, u32[]{:S(2)}) copy-start(bf16[1,1,4,32,1024]{4,3,2,1,0:T(8,128)(2,1)} %copy-done.2) | copy-start | bytes 786436
  302.0 23.9 %copy-start.5 = (bf16[1,1,4,32,1024]{4,3,2,1,0:T(8,128)(2,1)S(1)}, bf16[1,1,4,32,1024]{4,3,2,1,0:T(8,128)(2,1)}, u32[]{:S(2)}) copy-start(bf16[1,1,4,32,1024]{4,3,2,1,0:T(8,128)(2,1)} %copy-done.4) | copy-start | bytes 786436
  302.0 24.2 %copy-start.7 = (bf16[1,1,4,32,1024]{4,3,2,1,0:T(8,128)(2,1)S(1)}, bf16[1,1,4,32,1024]{4,3,2,1,0:T(8,128)(2,1)}, u32[]{:S(2)}) copy-start(bf16[1,1,4,32,1024]{4,3,2,1,0:T(8,128)(2,1)} %copy-done.6) | copy-start | bytes 786436
  302.1 24.6 %copy-start.9 = (bf16[1,1,4,32,1024]{4,3,2,1,0:T(8,128)(2,1)S(1)}, bf16[1,1,4,32,1024]{4,3,2,1,0:T(8,128)(2,1)}, u32[]{:S(2)}) copy-start(bf16[1,1,4,32,1024]{4,3,2,1,0:T(8,128)(2,1)} %copy-done.8) | copy-start | bytes 786436
  324.8 61.8 %copy-start.20 = (f32[1,4,16,64]{3,2,1,0:T(8,128)S(1)}, f32[1,4,16,64]{3,2,1,0:T(8,128)}, u32[]{:S(2)}) copy-start(f32[1,4,16,64]{3,2,1,0:T(8,128)} %param.13) | copy-start | bytes 49156
  (3 other events, 3.0 us)
Sparse Core Ops, SparseCore 0:
  14.2 32.8 all-gather.5
  161.4 41.4 reduce-scatter.2
  207.9 28.5 all-gather.7
  325.0 37.3 reduce-scatter.4
Sparse Core Ops, SparseCore 1:
  75.5 76.5 all-gather.9
